TPU v7x, 32 devices: a whole 2x2x4 slice. The times are simulated.
32 devices in a mesh: row: 4 (over x, core), col: 8 (over z, y).
Axes of the slice: x: 2, y: 2, z: 4, core: 2. Of those that a mesh axis runs over, the one named last changes fastest.
Arguments:
- right_side: float32 [64, 16384], P(None, 'row'), may hold values from -8 to 8
- blocks: bfloat16 [3072, 128, 128], P(('row', 'col')), may hold values from -1 to 1
- targets: int32 [3072, 1], P(('row', 'col')), may hold values from 0 to 7; in each aligned block of 96 rows (0 to 95, 96 to 191, ...) at most 24 rows name the same one
- tile_rows: int32 [3072], P(('row', 'col')), may hold values from 0 to 31
- tile_cols: int32 [3072], P(('row', 'col')), may hold values from 0 to 31
Outputs:
- solution: float32 [64, 8, 4096], P(None, 'col', 'row')
- phibar: float32 [64], replicated
Inputs may be any that keep to these rules, and one draw needn't show every extreme that they name: `targets`: among the 96 blocks of one device, at most 24 name the same grid column, and some grid column is named exactly 24 times by some device.
All inputs are finite; a program needn't handle non-finite values.
Results may differ from a plain program's by a relative error of at most 0.0032.
Values may be sent and summed in bfloat16 or wider, within the bound.
No kernel may reach another device: no remote copies, remote signals or barrier semaphores. Data moves between devices by JAX's collectives and lax.ppermute only.
A program may use at most 128 MiB of HBM per device.

v0:
```python
import jax
import jax.numpy as jnp
from jax import lax
from jax.sharding import PartitionSpec as P

TC = 32
ITERS = 4
EPSILON = 1e-06


def gather_tiles(vector_bf, indices, block_size):
    snapshots, extent = vector_bf.shape
    vector_tiles = vector_bf.reshape(snapshots, extent // block_size, block_size)
    return jnp.take(vector_tiles, indices, axis=1)


def place_terms(weighted, indices, n_out):
    snapshots, number, block_size = weighted.shape
    onehot = (indices[:, None] == jnp.arange(n_out, dtype=jnp.int32)[None, :]).astype(jnp.float32)
    summed = jnp.einsum("ksi,st->kti", weighted, onehot, precision=lax.Precision.HIGHEST)
    return summed.reshape(snapshots, n_out * block_size)


def forward_terms(vector_bf, blocks, row_index, col_index, n_out):
    picked = gather_tiles(vector_bf, col_index, blocks.shape[1])
    weighted = jnp.einsum("sij,ksj->ksi", blocks, picked, preferred_element_type=jnp.float32)
    return place_terms(weighted, row_index, n_out)


def backward_terms(vector_bf, blocks, row_index, col_index, n_out):
    picked = gather_tiles(vector_bf, row_index, blocks.shape[1])
    weighted = jnp.einsum("sji,ksj->ksi", blocks, picked, preferred_element_type=jnp.float32)
    return place_terms(weighted, col_index, n_out)


def per_device(right_side, blocks, targets, tile_rows, tile_cols):
    col_count = lax.axis_size("col")
    row_count = lax.axis_size("row")
    block_size = blocks.shape[1]
    snapshots = right_side.shape[0]
    row_tiles = right_side.shape[1] // block_size
    own_count = blocks.shape[0]
    capacity = 2 * own_count // col_count
    target = targets[:, 0]
    matches = (target[:, None] == jnp.arange(col_count, dtype=jnp.int32)[None, :]).astype(jnp.int32)
    before = jnp.cumsum(matches, axis=0) - matches
    slot_index = target * capacity + jnp.sum(before * matches, axis=1)
    outgoing = (
        jnp.zeros((col_count * capacity, block_size, block_size), blocks.dtype)
        .at[slot_index]
        .set(blocks)
    )
    places = (
        jnp.zeros((col_count * capacity, 2), jnp.int32)
        .at[slot_index]
        .set(jnp.stack([tile_rows, tile_cols], axis=1))
    )
    arrived, arrived_places = (
        lax.all_to_all(
            outgoing.reshape(col_count, capacity, block_size, block_size),
            "col",
            split_axis=0,
            concat_axis=0,
            tiled=True,
        ),
        lax.all_to_all(
            places.reshape(col_count, capacity, 2), "col", split_axis=0, concat_axis=0, tiled=True
        ),
    )
    work_blocks = arrived.reshape(col_count * capacity, block_size, block_size)
    flat_places = arrived_places.reshape(col_count * capacity, 2)
    work_rows = flat_places[:, 0]
    work_cols = flat_places[:, 1]

    def backward(left_bf):
        return backward_terms(left_bf, work_blocks, work_rows, work_cols, TC)

    def sum_right(partial_value):
        return lax.psum(partial_value, "row")

    def finish_left(unscaled, need_form):
        squares = jnp.sum(unscaled * unscaled, axis=1)
        total = lax.psum(squares, "row")
        beta_norm = jnp.sqrt(total + EPSILON)
        scaled = unscaled / beta_norm[:, None]
        rounded = None
        if need_form:
            rounded = scaled.astype(jnp.bfloat16)
        return (beta_norm, scaled, rounded)

    def finish_right(unscaled):
        squares = jnp.sum(unscaled * unscaled, axis=1)
        total = lax.psum(squares, "col")
        alpha_norm = jnp.sqrt(total + EPSILON)
        scaled = unscaled / alpha_norm[:, None]
        rounded = scaled.astype(jnp.bfloat16)
        return (alpha_norm, scaled, rounded)

    beta_norm, left_vec, left_bf = finish_left(right_side, True)
    alpha_norm, right_vec, right_bf = finish_right(sum_right(backward(left_bf)))
    search = right_vec
    solution = jnp.zeros_like(right_vec)
    phibar = beta_norm
    rhobar = alpha_norm
    for iteration in range(ITERS):
        last_turn = iteration + 1 == ITERS
        unscaled = (
            lax.psum(forward_terms(right_bf, work_blocks, work_rows, work_cols, row_tiles), "col")
            - alpha_norm[:, None] * left_vec
        )
        beta_norm, left_vec, left_bf = finish_left(unscaled, not last_turn)
        rho_value = jnp.sqrt(rhobar * rhobar + beta_norm * beta_norm)
        cosine = rhobar / rho_value
        sine_value = beta_norm / rho_value
        phi_value = cosine * phibar
        phibar = sine_value * phibar
        solution = solution + (phi_value / rho_value)[:, None] * search
        if not last_turn:
            unscaled = sum_right(backward(left_bf)) - beta_norm[:, None] * right_vec
            alpha_norm, right_vec, right_bf = finish_right(unscaled)
            theta_value = sine_value * alpha_norm
            rhobar = -cosine * alpha_norm
            search = right_vec - (theta_value / rho_value)[:, None] * search
    share_len = solution.shape[1] // row_count
    solution = lax.dynamic_slice_in_dim(solution, lax.axis_index("row") * share_len, share_len, 1)
    return (solution.reshape(snapshots, 1, solution.shape[1]), phibar)


def solution(mesh):
    placed = (
        P(None, "row"),
        P(("row", "col"), None, None),
        P(("row", "col"), None),
        P(("row", "col")),
        P(("row", "col")),
    )
    return jax.shard_map(
        per_device,
        mesh=mesh,
        in_specs=placed,
        out_specs=(P(None, "col", "row"), P()),
        check_vma=False,
    )
```

profile of v0, /device:TPU:0, one launch (start us, length us, event | category | flops | bytes accessed | tf_op | source)
XLA Modules:
  0.0 906.9 jit_solution(17280355181446882380)
XLA Ops:
  11.9 7.3 all-to-all-start
  23.4 14.7 %scatter_fusion = bf16[192,128,128]{2,1,0:T(8,128)(2,1)} fusion(bf16[192,128,128]{2,1,0:T(8,128)(2,1)} %broadcast_in_dim.14, s32[96]{0:T(128)S(1)} %fusion.105, bf16[96,128,128]{2,1,0:T(8,128)(2,1)} %param.8), kind=kCustom, calls=%fused_computation.9 | custom fusion | bytes 9437568 | tf_op jit(solution)/shard_map/scatter | solution.py:51
  38.1 6.1 all-to-all-start.1
  53.3 128.6 %all-to-all-done.1 = bf16[8,24,128,128]{3,2,1,0:T(8,128)(2,1)} async-done(((bf16[8,24,128,128]{3,2,1,0:T(8,128)(2,1)}), bf16[8,24,128,128]{3,2,1,0:T(8,128)(2,1)}, u32[]{:S(2)}, u32[]{:S(2)}) %all-to-all-start.1) | async-done | bytes 6291488 | tf_op jit(solution)/shard_map/all_to_all | solution.py:59
  194.9 35.2 %all-reduce.9.cloned.1.call-done = f32[64,4096]{1,0:T(8,128)} async-done(((f32[64,4096]{1,0:T(8,128)}), f32[64,4096]{1,0:T(8,128)}) %all-reduce.9.cloned.1.call-update) | async-done | bytes 1048592 | tf_op jit(solution)/shard_map/psum | solution.py:79
  231.5 21.5 %psum.121 = f32[64]{0:T(128)S(1)} all-reduce(f32[64]{0:T(128)S(1)} %multiply_reduce_fusion.7), channel_id=1, replica_groups=mesh['row'=4,'col'=8] {'col'}, use_global_device_ids=true, to_apply=%region_8.10 | all-reduce | flops 64 | bytes 512 | tf_op jit(solution)/shard_map/psum | solution.py:93
  257.4 8.1 fusion.51
  272.8 75.0 %all-reduce.11.cloned.1.call-done = f32[64,4096]{1,0:T(8,128)} async-done(((f32[64,4096]{1,0:T(8,128)}), f32[64,4096]{1,0:T(8,128)}) %all-reduce.11.cloned.1.call-update) | async-done | bytes 1048592 | tf_op jit(solution)/shard_map/psum | solution.py:108
  350.4 6.1 psum.123
  373.7 35.8 %all-reduce.13.cloned.1.call-done = f32[64,4096]{1,0:T(8,128)} async-done(((f32[64,4096]{1,0:T(8,128)}), f32[64,4096]{1,0:T(8,128)}) %all-reduce.13.cloned.1.call-update) | async-done | bytes 1048592 | tf_op jit(solution)/shard_map/psum | solution.py:79
  411.0 21.8 %psum.125 = f32[64]{0:T(128)S(1)} all-reduce(f32[64]{0:T(128)S(1)} %multiply_reduce_fusion.5), channel_id=1, replica_groups=mesh['row'=4,'col'=8] {'col'}, use_global_device_ids=true, to_apply=%region_14.16 | all-reduce | flops 64 | bytes 512 | tf_op jit(solution)/shard_map/psum | solution.py:93
  437.2 8.1 fusion.57
  452.8 75.0 %all-reduce.15.cloned.1.call-done = f32[64,4096]{1,0:T(8,128)} async-done(((f32[64,4096]{1,0:T(8,128)}), f32[64,4096]{1,0:T(8,128)}) %all-reduce.15.cloned.1.call-update) | async-done | bytes 1048592 | tf_op jit(solution)/shard_map/psum | solution.py:108
  530.3 6.1 psum.127
  553.6 35.8 %all-reduce.17.cloned.1.call-done = f32[64,4096]{1,0:T(8,128)} async-done(((f32[64,4096]{1,0:T(8,128)}), f32[64,4096]{1,0:T(8,128)}) %all-reduce.17.cloned.1.call-update) | async-done | bytes 1048592 | tf_op jit(solution)/shard_map/psum | solution.py:79
  591.0 21.6 %psum.129 = f32[64]{0:T(128)S(1)} all-reduce(f32[64]{0:T(128)S(1)} %multiply_reduce_fusion.3), channel_id=1, replica_groups=mesh['row'=4,'col'=8] {'col'}, use_global_device_ids=true, to_apply=%region_20.22 | all-reduce | flops 64 | bytes 512 | tf_op jit(solution)/shard_map/psum | solution.py:93
  617.9 8.1 fusion.63
  633.5 75.0 %all-reduce.19.cloned.1.call-done = f32[64,4096]{1,0:T(8,128)} async-done(((f32[64,4096]{1,0:T(8,128)}), f32[64,4096]{1,0:T(8,128)}) %all-reduce.19.cloned.1.call-update) | async-done | bytes 1048592 | tf_op jit(solution)/shard_map/psum | solution.py:108
  711.0 6.3 psum.131
  734.5 35.8 %all-reduce.21.cloned.1.call-done = f32[64,4096]{1,0:T(8,128)} async-done(((f32[64,4096]{1,0:T(8,128)}), f32[64,4096]{1,0:T(8,128)}) %all-reduce.21.cloned.1.call-update) | async-done | bytes 1048592 | tf_op jit(solution)/shard_map/psum | solution.py:79
  771.9 21.5 %psum.133 = f32[64]{0:T(128)S(1)} all-reduce(f32[64]{0:T(128)S(1)} %multiply_reduce_fusion.1), channel_id=1, replica_groups=mesh['row'=4,'col'=8] {'col'}, use_global_device_ids=true, to_apply=%region_26.28 | all-reduce | flops 64 | bytes 512 | tf_op jit(solution)/shard_map/psum | solution.py:93
  798.8 8.1 fusion.69
  814.4 75.1 %all-reduce.23.cloned.1.call-done = f32[64,4096]{1,0:T(8,128)} async-done(((f32[64,4096]{1,0:T(8,128)}), f32[64,4096]{1,0:T(8,128)}) %all-reduce.23.cloned.1.call-update) | async-done | bytes 1048592 | tf_op jit(solution)/shard_map/psum | solution.py:108
  891.0 5.9 psum.135
  (108 shorter events, 149.8 us)
Async XLA Ops:
  11.9 26.2 %all-to-all-start = ((s32[8,24,2]{1,2,0:T(2,128)}), s32[8,24,2]{1,2,0:T(2,128)S(1)}, u32[]{:S(2)}, u32[]{:S(2)}) async-start(s32[8,24,2]{1,2,0:T(2,128)} %copy.46), calls=%async_computation | async-start | bytes 16384 | tf_op jit(solution)/shard_map/all_to_all | solution.py:66
  38.1 6.1 copy-start.1
  38.1 143.8 %all-to-all-start.1 = ((bf16[8,24,128,128]{3,2,1,0:T(8,128)(2,1)}), bf16[8,24,128,128]{3,2,1,0:T(8,128)(2,1)}, u32[]{:S(2)}, u32[]{:S(2)}) async-start(bf16[8,24,128,128]{3,2,1,0:T(8,128)(2,1)} %bitcast.172), calls=%async_computation.1 | async-start | bytes 12582912 | tf_op jit(solution)/shard_map/all_to_all | solution.py:59
  44.2 185.9 %all-reduce.9.cloned.1.call-start = ((), (), s32[]{:S(2)}) async-start(), calls=%async_computation.2 | async-start | bytes 2097152 | tf_op jit(solution)/shard_map/psum | solution.py:79
  194.8 153.0 %all-reduce.11.cloned.1.call-start = ((), (), s32[]{:S(2)}) async-start(), calls=%async_computation.3 | async-start | bytes 2097152 | tf_op jit(solution)/shard_map/psum | solution.py:108
  272.8 136.7 %all-reduce.13.cloned.1.call-start = ((), (), s32[]{:S(2)}) async-start(), calls=%async_computation.4 | async-start | bytes 2097152 | tf_op jit(solution)/shard_map/psum | solution.py:79
  373.6 154.1 %all-reduce.15.cloned.1.call-start = ((), (), s32[]{:S(2)}) async-start(), calls=%async_computation.5 | async-start | bytes 2097152 | tf_op jit(solution)/shard_map/psum | solution.py:108
  451.1 76.6 %copy-start.4 = (f32[64,4096]{1,0:T(8,128)S(1)}, f32[64,4096]{1,0:T(8,128)}, u32[]{:S(2)}) copy-start(f32[64,4096]{1,0:T(8,128)} %get-tuple-element.25) | copy-start | bytes 3145732
  452.7 136.7 %all-reduce.17.cloned.1.call-start = ((), (), s32[]{:S(2)}) async-start(), calls=%async_computation.6 | async-start | bytes 2097152 | tf_op jit(solution)/shard_map/psum | solution.py:79
  553.5 154.9 %all-reduce.19.cloned.1.call-start = ((), (), s32[]{:S(2)}) async-start(), calls=%async_computation.7 | async-start | bytes 2097152 | tf_op jit(solution)/shard_map/psum | solution.py:108
  631.8 76.6 %copy-start.3 = (f32[64,4096]{1,0:T(8,128)S(1)}, f32[64,4096]{1,0:T(8,128)}, u32[]{:S(2)}) copy-start(f32[64,4096]{1,0:T(8,128)} %get-tuple-element.21) | copy-start | bytes 3145732
  633.4 136.9 %all-reduce.21.cloned.1.call-start = ((), (), s32[]{:S(2)}) async-start(), calls=%async_computation.8 | async-start | bytes 2097152 | tf_op jit(solution)/shard_map/psum | solution.py:79
  732.9 37.5 %copy-start = (f32[64,4096]{1,0:T(8,128)S(1)}, f32[64,4096]{1,0:T(8,128)}, u32[]{:S(2)}) copy-start(f32[64,4096]{1,0:T(8,128)} %get-tuple-element.19) | copy-start | bytes 3145732
  734.5 155.0 %all-reduce.23.cloned.1.call-start = ((), (), s32[]{:S(2)}) async-start(), calls=%async_computation.9 | async-start | bytes 2097152 | tf_op jit(solution)/shard_map/psum | solution.py:108
  812.7 76.8 %copy-start.2 = (f32[64,4096]{1,0:T(8,128)S(1)}, f32[64,4096]{1,0:T(8,128)}, u32[]{:S(2)}) copy-start(f32[64,4096]{1,0:T(8,128)} %get-tuple-element.17) | copy-start | bytes 3145732
Sparse Core Ops, SparseCore 0:
  194.9 35.0 all-reduce.8
  272.9 74.8 all-reduce.10
  373.7 35.7 all-reduce.12
  452.9 74.8 all-reduce.14
  553.7 35.7 all-reduce.16
  633.5 74.8 all-reduce.18
  734.6 35.7 all-reduce.20
  814.5 74.9 all-reduce.22
where the time goes:
time: 916 us; the launch traced here: 907 us
  waiting for transfers between devices  571 us (62%)
  blocking collectives  116 us (13%)
  matrix products  101 us (11%)
  local copies, waits for them, and re-layouts  56.9 us (6%)
  other arithmetic  32.9 us (4%)
  between operations  14.7 us (2%)
  starting transfers between devices  13.7 us (1%)
    psum x4, waiting for transfers between devices, per_device(): lax.psum(forward_terms(right_bf, work_blocks, work_rows, work_cols, row_t...  300 us
    psum x4, waiting for transfers between devices, sum_right(): return lax.psum(partial_value, 'row')  143 us
    all_to_all x1, waiting for transfers between devices, per_device(): lax.all_to_all(outgoing.reshape(col_count, capacity, block_size, block_si...  129 us
    psum x4, blocking collectives, finish_right(): total = lax.psum(squares, 'col')  86.4 us
    dot_general x8, matrix products, place_terms(): jnp.einsum('ksi,st->kti', weighted, onehot, precision=lax.Precision.HIGHEST)  46.2 us
    dot_general x4, matrix products, forward_terms(): jnp.einsum('sij,ksj->ksi', blocks, picked, preferred_element_type=jnp.flo...  32.3 us
    psum x5, blocking collectives, finish_left(): total = lax.psum(squares, 'row')  30.1 us
    dot_general x4, matrix products, backward_terms(): jnp.einsum('sji,ksj->ksi', blocks, picked, preferred_element_type=jnp.flo...  22.3 us
  transfers between devices with their start and end apart: 10, of which 9 were waited for; matrix products, arithmetic and copies ran while one was open for 2% of the time, Pallas kernels for 0%

commit v1 on v0

--- a/solution.py
+++ b/solution.py
@@ -6,6 +6,28 @@
 TC = 32
 ITERS = 4
 EPSILON = 1e-06
+
+
+def cut_along(x, dim, peers):
+    before, after = (x.shape[:dim], x.shape[dim + 1 :])
+    return jnp.moveaxis(x.reshape(*before, peers, -1, *after), dim, 0)
+
+
+def in_order(blocks, dim):
+    blocks = jnp.moveaxis(blocks, 0, dim)
+    dims = blocks.shape
+    return blocks.reshape(*dims[:dim], dims[dim] * dims[dim + 1], *dims[dim + 2 :])
+
+
+def exchange_directly(value, axis, split_dim, concat_dim):
+    size, place = (lax.axis_size(axis), lax.axis_index(axis))
+    pieces = cut_along(value, split_dim, size)
+    gathered = [pieces[place]]
+    for turn in range(1, size):
+        sent = pieces[(place + turn) % size]
+        gathered.append(lax.ppermute(sent, axis, [(i, (i + turn) % size) for i in range(size)]))
+    pieces = jnp.stack(gathered)[(place - jnp.arange(size)) % size]
+    return in_order(pieces, concat_dim)
 
 
 def gather_tiles(vector_bf, indices, block_size):
@@ -56,12 +78,8 @@
         .set(jnp.stack([tile_rows, tile_cols], axis=1))
     )
     arrived, arrived_places = (
-        lax.all_to_all(
-            outgoing.reshape(col_count, capacity, block_size, block_size),
-            "col",
-            split_axis=0,
-            concat_axis=0,
-            tiled=True,
+        exchange_directly(
+            outgoing.reshape(col_count, capacity, block_size, block_size), "col", 0, 0
         ),
         lax.all_to_all(
             places.reshape(col_count, capacity, 2), "col", split_axis=0, concat_axis=0, tiled=True

time: 916 us -> 933 us (1.019)
  local copies, waits for them, and re-layouts: 56.9 us -> 81 us
    all_to_all x1 -> x0, waiting for transfers between devices: 129 us -> none  [per_device(): lax.all_to_all(outgoing.reshape(col_count, capacity, block_size, block_si...]
    all_to_all x1, waiting for transfers between devices: 0.01 us -> 103 us  [per_device(): lax.all_to_all(places.reshape(col_count, capacity, 2), 'col', split_axis=...]
    ppermute x0 -> x7, waiting for transfers between devices: none -> 19.8 us  [exchange_directly(): lax.ppermute(sent, axis, [(i, (i + turn) % size) for i in range(size)])]
    ppermute x0 -> x7, starting transfers between devices: none -> 13.5 us  [exchange_directly(): lax.ppermute(sent, axis, [(i, (i + turn) % size) for i in range(size)])]
    unnamed x18 -> x36, local copies, waits for them, and re-layouts: 12.7 us -> 24.6 us
  transfers between devices with their start and end apart: 10 -> 16, of which waited for: 9 -> 11; matrix products, arithmetic and copies ran while one was open for 2% -> 2% of each run, Pallas kernels for 0% -> 0%
where the time goes in v1:
time: 933 us; the launch traced here: 927 us
  waiting for transfers between devices  568 us (61%)
  blocking collectives  117 us (13%)
  matrix products  99.2 us (11%)
  local copies, waits for them, and re-layouts  81 us (9%)
  other arithmetic  30.4 us (3%)
  starting transfers between devices  17.2 us (2%)
  between operations  14.8 us (2%)
    psum x4, waiting for transfers between devices, per_device(): lax.psum(forward_terms(right_bf, work_blocks, work_rows, work_cols, row_t...  300 us
    psum x4, waiting for transfers between devices, sum_right(): return lax.psum(partial_value, 'row')  146 us
    all_to_all x1, waiting for transfers between devices, per_device(): lax.all_to_all(places.reshape(col_count, capacity, 2), 'col', split_axis=...  103 us
    psum x4, blocking collectives, finish_right(): total = lax.psum(squares, 'col')  86.4 us
    dot_general x8, matrix products, place_terms(): jnp.einsum('ksi,st->kti', weighted, onehot, precision=lax.Precision.HIGHEST)  46.4 us
    dot_general x4, matrix products, forward_terms(): jnp.einsum('sij,ksj->ksi', blocks, picked, preferred_element_type=jnp.flo...  32.3 us
    psum x5, blocking collectives, finish_left(): total = lax.psum(squares, 'row')  30.4 us
    unnamed x36, local copies, waits for them, and re-layouts  24.6 us
  transfers between devices with their start and end apart: 16, of which 11 were waited for; matrix products, arithmetic and copies ran while one was open for 2% of the time, Pallas kernels for 0%

profile of v1, /device:TPU:0, one launch (start us, length us, event | category | flops | bytes accessed | tf_op | source)
XLA Modules:
  0.0 927.4 jit_solution(14666452442117234669)
XLA Ops:
  14.0 12.7 %scatter_fusion = bf16[192,128,128]{2,1,0:T(8,128)(2,1)} fusion(bf16[192,128,128]{2,1,0:T(8,128)(2,1)} %broadcast_in_dim.14, s32[96]{0:T(128)S(1)} %fusion.106, bf16[96,128,128]{2,1,0:T(8,128)(2,1)S(1)} %copy-done.8), kind=kCustom, calls=%fused_computation.10 | custom fusion | bytes 9437568 | tf_op jit(solution)/shard_map/scatter | solution.py:73
  26.7 6.3 dynamic-slice_bitcast_fusion
  55.5 102.6 %all-to-all-done = s32[8,24,2]{1,2,0:T(2,128)S(1)} async-done(((s32[8,24,2]{1,2,0:T(2,128)}), s32[8,24,2]{1,2,0:T(2,128)S(1)}, u32[]{:S(2)}, u32[]{:S(2)}) %all-to-all-start) | async-done | bytes 1568 | tf_op jit(solution)/shard_map/all_to_all | solution.py:84
  174.2 7.3 collective-permute-done.5
  182.4 12.5 %collective-permute-done.6 = bf16[1,24,128,128]{3,2,1,0:T(8,128)(2,1)S(1)} collective-permute-done((bf16[1,24,128,128]{3,2,1,0:T(8,128)(2,1)S(1)}, bf16[1,24,128,128]{3,2,1,0:T(8,128)(2,1)S(1)}, u32[]{:S(2)}, u32[]{:S(2)}) %collective-permute-start.6) | collective-permute-done | bytes 786464 | tf_op jit(solution)/shard_map/ppermute | solution.py:28
  195.9 6.9 gather_fusion
  214.2 38.0 %all-reduce.9.cloned.1.call-done = f32[64,4096]{1,0:T(8,128)} async-done(((f32[64,4096]{1,0:T(8,128)}), f32[64,4096]{1,0:T(8,128)}) %all-reduce.9.cloned.1.call-update) | async-done | bytes 1048592 | tf_op jit(solution)/shard_map/psum | solution.py:97
  253.7 21.5 %psum.121 = f32[64]{0:T(128)S(1)} all-reduce(f32[64]{0:T(128)S(1)} %multiply_reduce_fusion.7), channel_id=1, replica_groups=mesh['row'=4,'col'=8] {'col'}, use_global_device_ids=true, to_apply=%region_8.10 | all-reduce | flops 64 | bytes 512 | tf_op jit(solution)/shard_map/psum | solution.py:111
  279.6 8.1 fusion.51
  295.2 75.0 %all-reduce.11.cloned.1.call-done = f32[64,4096]{1,0:T(8,128)} async-done(((f32[64,4096]{1,0:T(8,128)}), f32[64,4096]{1,0:T(8,128)}) %all-reduce.11.cloned.1.call-update) | async-done | bytes 1048592 | tf_op jit(solution)/shard_map/psum | solution.py:126
  371.8 6.1 psum.123
  393.9 35.8 %all-reduce.13.cloned.1.call-done = f32[64,4096]{1,0:T(8,128)} async-done(((f32[64,4096]{1,0:T(8,128)}), f32[64,4096]{1,0:T(8,128)}) %all-reduce.13.cloned.1.call-update) | async-done | bytes 1048592 | tf_op jit(solution)/shard_map/psum | solution.py:97
  431.3 21.8 %psum.125 = f32[64]{0:T(128)S(1)} all-reduce(f32[64]{0:T(128)S(1)} %multiply_reduce_fusion.5), channel_id=1, replica_groups=mesh['row'=4,'col'=8] {'col'}, use_global_device_ids=true, to_apply=%region_14.16 | all-reduce | flops 64 | bytes 512 | tf_op jit(solution)/shard_map/psum | solution.py:111
  457.5 8.1 fusion.57
  473.1 74.9 %all-reduce.15.cloned.1.call-done = f32[64,4096]{1,0:T(8,128)} async-done(((f32[64,4096]{1,0:T(8,128)}), f32[64,4096]{1,0:T(8,128)}) %all-reduce.15.cloned.1.call-update) | async-done | bytes 1048592 | tf_op jit(solution)/shard_map/psum | solution.py:126
  573.8 35.8 %all-reduce.17.cloned.1.call-done = f32[64,4096]{1,0:T(8,128)} async-done(((f32[64,4096]{1,0:T(8,128)}), f32[64,4096]{1,0:T(8,128)}) %all-reduce.17.cloned.1.call-update) | async-done | bytes 1048592 | tf_op jit(solution)/shard_map/psum | solution.py:97
  611.2 21.6 %psum.129 = f32[64]{0:T(128)S(1)} all-reduce(f32[64]{0:T(128)S(1)} %multiply_reduce_fusion.3), channel_id=1, replica_groups=mesh['row'=4,'col'=8] {'col'}, use_global_device_ids=true, to_apply=%region_20.22 | all-reduce | flops 64 | bytes 512 | tf_op jit(solution)/shard_map/psum | solution.py:111
  638.2 8.1 fusion.63
  653.8 75.0 %all-reduce.19.cloned.1.call-done = f32[64,4096]{1,0:T(8,128)} async-done(((f32[64,4096]{1,0:T(8,128)}), f32[64,4096]{1,0:T(8,128)}) %all-reduce.19.cloned.1.call-update) | async-done | bytes 1048592 | tf_op jit(solution)/shard_map/psum | solution.py:126
  731.3 6.3 psum.131
  755.0 35.8 %all-reduce.21.cloned.1.call-done = f32[64,4096]{1,0:T(8,128)} async-done(((f32[64,4096]{1,0:T(8,128)}), f32[64,4096]{1,0:T(8,128)}) %all-reduce.21.cloned.1.call-update) | async-done | bytes 1048592 | tf_op jit(solution)/shard_map/psum | solution.py:97
  792.4 21.5 %psum.133 = f32[64]{0:T(128)S(1)} all-reduce(f32[64]{0:T(128)S(1)} %multiply_reduce_fusion.1), channel_id=1, replica_groups=mesh['row'=4,'col'=8] {'col'}, use_global_device_ids=true, to_apply=%region_26.28 | all-reduce | flops 64 | bytes 512 | tf_op jit(solution)/shard_map/psum | solution.py:111
  819.3 8.1 fusion.69
  834.9 75.1 %all-reduce.23.cloned.1.call-done = f32[64,4096]{1,0:T(8,128)} async-done(((f32[64,4096]{1,0:T(8,128)}), f32[64,4096]{1,0:T(8,128)}) %all-reduce.23.cloned.1.call-update) | async-done | bytes 1048592 | tf_op jit(solution)/shard_map/psum | solution.py:126
  (143 shorter events, 187.8 us)
Async XLA Ops:
  26.7 17.2 %copy-start.9 = (s32[96]{0:T(128)S(1)}, s32[96]{0:T(128)}, u32[]{:S(2)}) copy-start(s32[96]{0:T(128)} %param.11) | copy-start | bytes 1156
  26.7 17.2 %copy-start.10 = (s32[96]{0:T(128)S(1)}, s32[96]{0:T(128)}, u32[]{:S(2)}) copy-start(s32[96]{0:T(128)} %param.10) | copy-start | bytes 1156
  26.7 22.2 %copy-start.2 = (f32[64,4096]{1,0:T(8,128)S(1)}, f32[64,4096]{1,0:T(8,128)}, u32[]{:S(2)}) copy-start(f32[64,4096]{1,0:T(8,128)} %param.7) | copy-start | bytes 3145732
  33.0 127.9 %collective-permute-start = (bf16[1,24,128,128]{3,2,1,0:T(8,128)(2,1)}, bf16[1,24,128,128]{3,2,1,0:T(8,128)(2,1)}, u32[]{:S(2)}, u32[]{:S(2)}) collective-permute-start(bf16[1,24,128,128]{3,2,1,0:T(8,128)(2,1)} %get-tuple-element.34), channel_id=1, source_target_pairs={{0,1},{1,2},{2,3},{3,4},{4,5},{5,6},{6,7},{7,0},{8,9},{9,10},{10,1... | collective-permute-start | bytes 2359304 | tf_op jit(solution)/shard_map/ppermute | solution.py:28
  36.0 128.5 %collective-permute-start.1 = (bf16[1,24,128,128]{3,2,1,0:T(8,128)(2,1)}, bf16[1,24,128,128]{3,2,1,0:T(8,128)(2,1)}, u32[]{:S(2)}, u32[]{:S(2)}) collective-permute-start(bf16[1,24,128,128]{3,2,1,0:T(8,128)(2,1)} %get-tuple-element.33), channel_id=1, source_target_pairs={{0,2},{1,3},{2,4},{3,5},{4,6},{5,7},{6,0},{7,1},{8,10},{9,11},{10,... | collective-permute-start | bytes 2359304 | tf_op jit(solution)/shard_map/ppermute | solution.py:28
  37.5 130.2 %collective-permute-start.2 = (bf16[1,24,128,128]{3,2,1,0:T(8,128)(2,1)}, bf16[1,24,128,128]{3,2,1,0:T(8,128)(2,1)}, u32[]{:S(2)}, u32[]{:S(2)}) collective-permute-start(bf16[1,24,128,128]{3,2,1,0:T(8,128)(2,1)} %get-tuple-element.32), channel_id=1, source_target_pairs={{0,3},{1,4},{2,5},{3,6},{4,7},{5,0},{6,1},{7,2},{8,11},{9,12},{10,... | collective-permute-start | bytes 2359304 | tf_op jit(solution)/shard_map/ppermute | solution.py:28
  40.1 129.9 %collective-permute-start.3 = (bf16[1,24,128,128]{3,2,1,0:T(8,128)(2,1)}, bf16[1,24,128,128]{3,2,1,0:T(8,128)(2,1)}, u32[]{:S(2)}, u32[]{:S(2)}) collective-permute-start(bf16[1,24,128,128]{3,2,1,0:T(8,128)(2,1)} %get-tuple-element.31), channel_id=1, source_target_pairs={{0,4},{1,5},{2,6},{3,7},{4,0},{5,1},{6,2},{7,3},{8,12},{9,13},{10,... | collective-permute-start | bytes 2359304 | tf_op jit(solution)/shard_map/ppermute | solution.py:28
  41.2 130.8 %collective-permute-start.4 = (bf16[1,24,128,128]{3,2,1,0:T(8,128)(2,1)}, bf16[1,24,128,128]{3,2,1,0:T(8,128)(2,1)}, u32[]{:S(2)}, u32[]{:S(2)}) collective-permute-start(bf16[1,24,128,128]{3,2,1,0:T(8,128)(2,1)} %get-tuple-element.30), channel_id=1, source_target_pairs={{0,5},{1,6},{2,7},{3,0},{4,1},{5,2},{6,3},{7,4},{8,13},{9,14},{10,... | collective-permute-start | bytes 2359304 | tf_op jit(solution)/shard_map/ppermute | solution.py:28
  45.6 112.5 %all-to-all-start = ((s32[8,24,2]{1,2,0:T(2,128)}), s32[8,24,2]{1,2,0:T(2,128)S(1)}, u32[]{:S(2)}, u32[]{:S(2)}) async-start(s32[8,24,2]{1,2,0:T(2,128)} %copy.46), calls=%async_computation | async-start | bytes 16384 | tf_op jit(solution)/shard_map/all_to_all | solution.py:84
  48.9 203.4 %all-reduce.9.cloned.1.call-start = ((), (), s32[]{:S(2)}) async-start(), calls=%async_computation.1 | async-start | bytes 2097152 | tf_op jit(solution)/shard_map/psum | solution.py:97
  160.9 20.5 %collective-permute-start.5 = (bf16[1,24,128,128]{3,2,1,0:T(8,128)(2,1)S(1)}, bf16[1,24,128,128]{3,2,1,0:T(8,128)(2,1)S(1)}, u32[]{:S(2)}, u32[]{:S(2)}) collective-permute-start(bf16[1,24,128,128]{3,2,1,0:T(8,128)(2,1)S(1)} %get-tuple-element.29), channel_id=1, source_target_pairs={{0,6},{1,7},{2,0},{3,1},{4,2},{5,3},{6,4},{7,5},{8,14},{9,15},{10,... | collective-permute-start | bytes 2359304 | tf_op jit(solution)/shard_map/ppermute | solution.py:28
  164.5 30.4 %collective-permute-start.6 = (bf16[1,24,128,128]{3,2,1,0:T(8,128)(2,1)S(1)}, bf16[1,24,128,128]{3,2,1,0:T(8,128)(2,1)S(1)}, u32[]{:S(2)}, u32[]{:S(2)}) collective-permute-start(bf16[1,24,128,128]{3,2,1,0:T(8,128)(2,1)S(1)} %get-tuple-element.28), channel_id=1, source_target_pairs={{0,7},{1,0},{2,1},{3,2},{4,3},{5,4},{6,5},{7,6},{8,15},{9,8},{10,9... | collective-permute-start | bytes 2359304 | tf_op jit(solution)/shard_map/ppermute | solution.py:28
  214.2 156.0 %all-reduce.11.cloned.1.call-start = ((), (), s32[]{:S(2)}) async-start(), calls=%async_computation.2 | async-start | bytes 2097152 | tf_op jit(solution)/shard_map/psum | solution.py:126
  287.7 82.5 %copy-start.3 = (f32[64,4096]{1,0:T(8,128)S(1)}, f32[64,4096]{1,0:T(8,128)}, u32[]{:S(2)}) copy-start(f32[64,4096]{1,0:T(8,128)} %param.7) | copy-start | bytes 3145732
  295.1 134.7 %all-reduce.13.cloned.1.call-start = ((), (), s32[]{:S(2)}) async-start(), calls=%async_computation.3 | async-start | bytes 2097152 | tf_op jit(solution)/shard_map/psum | solution.py:97
  393.9 154.0 %all-reduce.15.cloned.1.call-start = ((), (), s32[]{:S(2)}) async-start(), calls=%async_computation.4 | async-start | bytes 2097152 | tf_op jit(solution)/shard_map/psum | solution.py:126
  465.6 82.4 %copy-start.7 = (f32[64,4096]{1,0:T(8,128)S(1)}, f32[64,4096]{1,0:T(8,128)}, u32[]{:S(2)}) copy-start(f32[64,4096]{1,0:T(8,128)} %copy-done.6) | copy-start | bytes 3145732
  473.0 136.7 %all-reduce.17.cloned.1.call-start = ((), (), s32[]{:S(2)}) async-start(), calls=%async_computation.5 | async-start | bytes 2097152 | tf_op jit(solution)/shard_map/psum | solution.py:97
  573.8 155.0 %all-reduce.19.cloned.1.call-start = ((), (), s32[]{:S(2)}) async-start(), calls=%async_computation.6 | async-start | bytes 2097152 | tf_op jit(solution)/shard_map/psum | solution.py:126
  646.3 82.5 %copy-start.5 = (f32[64,4096]{1,0:T(8,128)S(1)}, f32[64,4096]{1,0:T(8,128)}, u32[]{:S(2)}) copy-start(f32[64,4096]{1,0:T(8,128)} %get-tuple-element.21) | copy-start | bytes 3145732
  653.8 137.1 %all-reduce.21.cloned.1.call-start = ((), (), s32[]{:S(2)}) async-start(), calls=%async_computation.7 | async-start | bytes 2097152 | tf_op jit(solution)/shard_map/psum | solution.py:97
  747.5 43.4 %copy-start.1 = (f32[64,4096]{1,0:T(8,128)S(1)}, f32[64,4096]{1,0:T(8,128)}, u32[]{:S(2)}) copy-start(f32[64,4096]{1,0:T(8,128)} %get-tuple-element.19) | copy-start | bytes 3145732
  755.0 155.0 %all-reduce.23.cloned.1.call-start = ((), (), s32[]{:S(2)}) async-start(), calls=%async_computation.8 | async-start | bytes 2097152 | tf_op jit(solution)/shard_map/psum | solution.py:126
  827.4 82.6 %copy-start.4 = (f32[64,4096]{1,0:T(8,128)S(1)}, f32[64,4096]{1,0:T(8,128)}, u32[]{:S(2)}) copy-start(f32[64,4096]{1,0:T(8,128)} %get-tuple-element.17) | copy-start | bytes 3145732
  (3 other events, 28.5 us)
Sparse Core Ops, SparseCore 0:
  214.3 37.9 all-reduce.8
  295.2 74.8 all-reduce.10
  394.0 35.7 all-reduce.12
  473.1 74.7 all-reduce.14
  573.9 35.7 all-reduce.16
  653.9 74.8 all-reduce.18
  755.1 35.7 all-reduce.20
  835.0 74.9 all-reduce.22
